TPU v7x, 512 devices: a whole 4x4x16 slice. The times are simulated.
512 devices in a mesh: req: 128 (over x, z, core), head: 4 (over y).
Axes of the slice: x: 4, y: 4, z: 16, core: 2. Of those that a mesh axis runs over, the one named last changes fastest.
Arguments:
- queries: bfloat16 [128, 16, 2048], P('req', None, 'head'), may hold values from -6 to 6
- forget_logits: bfloat16 [128, 16, 2048], P('req', None, 'head'), may hold values from -8 to 8
- values: bfloat16 [128, 16, 2048], P('req', None, 'head'), may hold values from -6 to 6
- gate_input: bfloat16 [128, 16, 2048], P('req', None, 'head'), may hold values from -6 to 6
- init_states: float32 [128, 16, 128, 128], P('req', 'head'), may hold values from -4 to 4
- norm_gain: float32 [128], replicated, may hold values from 0.1 to 1.9
- out_weight: bfloat16 [2048, 2048], P('head'), may hold values from -0.125 to 0.125
- dealing: int32 [128], P('req'), may hold values from 0 to 127, as said below
- accepted: int32 [128], P('req'), may hold values from 0 to 16, as said below
Outputs:
- verified: bfloat16 [128, 16, 2048], P('req', None, 'head')
- new_states: float32 [128, 16, 128, 128], P('req', 'head')
Inputs may be any that keep to these rules, and one draw needn't show every extreme that they name: `dealing`: each request appears in exactly one dealt slot. `accepted`: some request accepts all 16 draft tokens and some accepts none.
All inputs are finite; a program needn't handle non-finite values.
Results may differ from a plain program's by a relative error of at most 0.0049.
Values may be sent and summed in bfloat16 or wider, within the bound.
No kernel may reach another device: no remote copies, remote signals or barrier semaphores. Data moves between devices by JAX's collectives and lax.ppermute only.
A program may use at most 64 MiB of HBM per device.

v0:
```python
import jax
import jax.numpy as jnp
from jax import lax
from jax.sharding import PartitionSpec as P

lower_bound = 0.8
norm_eps = 1e-05


def route_gathered(token_tuple, deal_all, worker, local_count):
    mine = worker * local_count + jnp.arange(local_count, dtype=jnp.int32)
    shard_rows = (
        lax.all_gather(token_tuple[0], "req", axis=0, tiled=True),
        lax.all_gather(token_tuple[1], "req", axis=0, tiled=True),
        lax.all_gather(token_tuple[2], "req", axis=0, tiled=True),
        lax.all_gather(token_tuple[3], "req", axis=0, tiled=True),
    )
    match = (deal_all[None, :] == mine[:, None]).astype(jnp.bfloat16)
    totals = tuple(
        (
            jnp.einsum("rk,kte->rte", match, rows, preferred_element_type=jnp.float32)
            for rows in shard_rows
        )
    )
    return tuple((acc.astype(jnp.bfloat16) for acc in totals))


def per_device(
    queries,
    forget_logits,
    values,
    gate_input,
    init_states,
    norm_gain,
    out_weight,
    dealing,
    accepted,
):
    local_count = queries.shape[0]
    draft_len = queries.shape[1]
    head_local = init_states.shape[1]
    head_size = init_states.shape[3]
    deal_all = lax.all_gather(dealing, "req", axis=0, tiled=True)
    worker = lax.axis_index("req")
    token_tuple = (queries, forget_logits, values, gate_input)
    tokens_q, tokens_f, tokens_v, tokens_g = route_gathered(
        token_tuple, deal_all, worker, local_count
    )

    def heads_of(tensor):
        return jnp.moveaxis(
            tensor.astype(jnp.float32).reshape(local_count, draft_len, head_local, head_size), 1, 0
        )

    query_seq = heads_of(tokens_q)
    forget_seq = lower_bound + (1.0 - lower_bound) * jax.nn.sigmoid(heads_of(tokens_f))
    value_seq = heads_of(tokens_v)
    numbers = jnp.arange(1, draft_len + 1, dtype=jnp.int32)

    def advance(state_pair, inputs):
        current, chosen = state_pair
        query_now, forget_now, value_now, number = inputs
        current = (
            forget_now[..., None] * current
            + (1.0 - forget_now)[..., None] * value_now[..., None, :]
        )
        chosen = jnp.where((accepted == number)[:, None, None, None], current, chosen)
        output = jnp.einsum("rhk,rhkv->rhv", query_now, current, precision=lax.Precision.HIGHEST)
        return ((current, chosen), output)

    (last_state, new_states), outputs = lax.scan(
        advance, (init_states, init_states), (query_seq, forget_seq, value_seq, numbers)
    )
    outputs = jnp.moveaxis(outputs, 0, 1)
    meansq = jnp.mean(outputs * outputs, axis=-1, keepdims=True)
    gate_heads = tokens_g.astype(jnp.float32).reshape(local_count, draft_len, head_local, head_size)
    mixed_rows = (
        outputs * lax.rsqrt(meansq + norm_eps) * norm_gain * jax.nn.silu(gate_heads)
    ).astype(jnp.bfloat16)
    mixed_rows = mixed_rows.reshape(local_count * draft_len, head_local * head_size)
    partial_out = jnp.dot(mixed_rows, out_weight, preferred_element_type=jnp.float32)
    summed = lax.psum_scatter(partial_out, "head", scatter_dimension=1, tiled=True)
    verified = summed.astype(jnp.bfloat16).reshape(local_count, draft_len, summed.shape[1])
    return (verified, new_states)


def solution(mesh):
    placed = (
        P("req", None, "head"),
        P("req", None, "head"),
        P("req", None, "head"),
        P("req", None, "head"),
        P("req", "head", None, None),
        P(),
        P("head", None),
        P("req"),
        P("req"),
    )
    return jax.shard_map(
        per_device,
        mesh=mesh,
        in_specs=placed,
        out_specs=(P("req", None, "head"), P("req", "head", None, None)),
        check_vma=False,
    )
```

profile of v0, /device:TPU:2, one launch (start us, length us, event | category | flops | bytes accessed | tf_op | source)
XLA Modules:
  0.0 614.6 jit_solution(16999576388277183235)
XLA Ops:
  7.2 1.1 copy.69
  8.4 0.7 all-gather.9.cloned.1.call-update
  9.1 0.7 all-gather.5.cloned.1.call-update
  9.9 0.5 all-gather.11.cloned.1.call-update
  11.1 1.3 dynamic-slice
  12.4 0.8 dynamic-update-slice
  13.2 33.1 %all-reduce = s32[128]{0:T(128)S(1)} all-reduce(s32[128]{0:T(128)S(1)} %dynamic-update-slice), channel_id=1, replica_groups=mesh['req'=128,'head'=4] {'req'}, use_global_device_ids=true, to_apply=%add | all-reduce | flops 128 | bytes 1024
  46.3 0.7 broadcast_bitcast_fusion
  46.9 108.4 %all-gather.7.cloned.1.call-done = bf16[128,16,512]{2,1,0:T(8,128)(2,1)} async-done(((bf16[1,16,512]{2,1,0:T(8,128)(2,1)}), bf16[128,16,512]{2,1,0:T(8,128)(2,1)}) %all-gather.7.cloned.1.call-update) | async-done | bytes 2097168 | tf_op jit(solution)/shard_map/all_gather | solution.py:15
  155.3 3.9 fusion.6
  159.2 136.3 %all-gather.9.cloned.1.call-done = bf16[128,16,512]{2,1,0:T(8,128)(2,1)} async-done(((bf16[1,16,512]{2,1,0:T(8,128)(2,1)}), bf16[128,16,512]{2,1,0:T(8,128)(2,1)}) %all-gather.9.cloned.1.call-update) | async-done | bytes 2097168 | tf_op jit(solution)/shard_map/all_gather | solution.py:13
  295.5 3.9 fusion.4
  299.4 136.3 %all-gather.5.cloned.1.call-done = bf16[128,16,512]{2,1,0:T(8,128)(2,1)} async-done(((bf16[1,16,512]{2,1,0:T(8,128)(2,1)}), bf16[128,16,512]{2,1,0:T(8,128)(2,1)}) %all-gather.5.cloned.1.call-update) | async-done | bytes 2097168 | tf_op jit(solution)/shard_map/all_gather | solution.py:14
  435.7 3.9 fusion.8
  439.7 40.8 %while.14 = (s32[]{:T(128)}, f32[1,4,128,128]{3,2,1,0:T(8,128)S(1)}, f32[1,4,128,128]{3,2,1,0:T(8,128)S(1)}, f32[16,1,4,128]{3,2,1,0:T(4,128)S(1)}, f32[16,1,4,1...) while((s32[]{:T(128)}, ...), condition=%wide.region_1.2_spmd, body=%wide.region_0.1_spmd.sunk | while | flops 1049091 | bytes 1339531 | solution.py:71
  439.7 0.6 dynamic_slice.23
  441.9 0.3 fusion.34
  442.2 0.6 dynamic_slice.23
  444.4 0.3 fusion.34
  444.8 0.6 dynamic_slice.23
  447.0 0.3 fusion.34
  447.3 0.6 dynamic_slice.23
  449.9 0.6 dynamic_slice.23
  452.1 0.3 fusion.34
  452.4 0.6 dynamic_slice.23
  454.6 0.3 fusion.34
  455.0 0.6 dynamic_slice.23
  457.2 0.3 fusion.34
  457.5 0.6 dynamic_slice.23
  459.7 0.3 fusion.34
  460.1 0.6 dynamic_slice.23
  462.3 0.3 fusion.34
  462.6 0.6 dynamic_slice.23
  464.8 0.3 fusion.34
  465.2 0.6 dynamic_slice.23
  467.4 0.3 fusion.34
  467.7 0.6 dynamic_slice.23
  469.9 0.3 fusion.34
  470.2 0.6 dynamic_slice.23
  472.8 0.6 dynamic_slice.23
  475.3 0.6 dynamic_slice.23
  477.6 0.3 fusion.34
  477.9 0.6 dynamic_slice.23
  480.6 95.3 %all-gather.11.cloned.1.call-done = bf16[128,16,512]{2,1,0:T(8,128)(2,1)} async-done(((bf16[1,16,512]{2,1,0:T(8,128)(2,1)}), bf16[128,16,512]{2,1,0:T(8,128)(2,1)}) %all-gather.11.cloned.1.call-update) | async-done | bytes 2097168 | tf_op jit(solution)/shard_map/all_gather | solution.py:16
  575.9 3.9 fusion.2
  579.8 1.0 fusion.16
  580.9 25.8 %reduce-scatter.2.cloned.1.call-done = f32[16,512]{1,0:T(8,128)} async-done(((f32[16,2048]{1,0:T(8,128)}), f32[16,512]{1,0:T(8,128)}) %reduce-scatter.2.cloned.1.call-update) | async-done | bytes 32784 | tf_op jit(solution)/shard_map/reduce_scatter | solution.py:82
  606.7 1.4 convert_bitcast_fusion
  (108 shorter events, 6.8 us)
Async XLA Ops:
  7.2 572.6 %copy-start = (bf16[512,2048]{1,0:T(8,128)(2,1)S(1)}, bf16[512,2048]{1,0:T(8,128)(2,1)}, u32[]{:S(2)}) copy-start(bf16[512,2048]{1,0:T(8,128)(2,1)} %param.17) | copy-start | bytes 6291460
  7.2 148.1 %all-gather.7.cloned.1.call-start = ((), (), s32[]{:S(2)}) async-start(), calls=%async_computation.2 | async-start | bytes 2113536 | tf_op jit(solution)/shard_map/all_gather | solution.py:15
  8.3 287.2 %all-gather.9.cloned.1.call-start = ((), (), s32[]{:S(2)}) async-start(), calls=%async_computation.3 | async-start | bytes 2113536 | tf_op jit(solution)/shard_map/all_gather | solution.py:13
  9.1 426.6 %all-gather.5.cloned.1.call-start = ((), (), s32[]{:S(2)}) async-start(), calls=%async_computation.1 | async-start | bytes 2113536 | tf_op jit(solution)/shard_map/all_gather | solution.py:14
  9.8 566.0 %all-gather.11.cloned.1.call-start = ((), (), s32[]{:S(2)}) async-start(), calls=%async_computation.4 | async-start | bytes 2113536 | tf_op jit(solution)/shard_map/all_gather | solution.py:16
  10.4 596.3 %reduce-scatter.2.cloned.1.call-start = ((), (), s32[]{:S(2)}) async-start(), calls=%async_computation.5 | async-start | bytes 163840 | tf_op jit(solution)/shard_map/reduce_scatter | solution.py:82
  480.4 100.4 %copy-start.1 = (f32[1,4,128,128]{3,2,1,0:T(8,128)}, f32[1,4,128,128]{3,2,1,0:T(8,128)S(1)}, u32[]{:S(2)}) copy-start(f32[1,4,128,128]{3,2,1,0:T(8,128)S(1)} %get-tuple-element.49) | copy-start | bytes 786436
Sparse Core Ops, SparseCore 0:
  11.1 144.1 all-gather.6
  158.4 137.0 all-gather.8
  298.7 137.0 all-gather.4
  438.7 137.0 all-gather.10
  581.0 25.6 reduce-scatter.1
where the time goes:
time: 615 us
  waiting for transfers between devices  504 us (82%)
  blocking collectives  33.1 us (5%)
  matrix products  21.6 us (4%)
  loops' own time  21.3 us (3%)
  between operations  14.5 us (2%)
  local copies, waits for them, and re-layouts  13.8 us (2%)
    all_gather x1, waiting for transfers between devices, route_gathered(): lax.all_gather(token_tuple[1], 'req', axis=0, tiled=True)  136 us
    all_gather x1, waiting for transfers between devices, route_gathered(): lax.all_gather(token_tuple[0], 'req', axis=0, tiled=True)  136 us
    all_gather x1, waiting for transfers between devices, route_gathered(): lax.all_gather(token_tuple[2], 'req', axis=0, tiled=True)  108 us
    all_gather x1, waiting for transfers between devices, route_gathered(): lax.all_gather(token_tuple[3], 'req', axis=0, tiled=True)  95.3 us
    unnamed x1, blocking collectives  33.1 us
    reduce_scatter x1, waiting for transfers between devices, per_device(): lax.psum_scatter(partial_out, 'head', scatter_dimension=1, tiled=True)  25.8 us
    another operation x1, loops' own time, per_device(): lax.scan(advance, (init_states, init_states), (query_seq, forget_seq, val...  21.3 us
    dot_general x4, matrix products, route_gathered(): jnp.einsum('rk,kte->rte', match, rows, preferred_element_type=jnp.float32)  15.5 us
  transfers between devices with their start and end apart: 5, of which 5 were waited for; matrix products, arithmetic and copies ran while one was open for 6% of the time, Pallas kernels for 0%

commit v1 on v0

--- a/solution.py
+++ b/solution.py
@@ -12,7 +12,9 @@
     shard_rows = (
         lax.all_gather(token_tuple[0], "req", axis=0, tiled=True),
         lax.all_gather(token_tuple[1], "req", axis=0, tiled=True),
-        lax.all_gather(token_tuple[2], "req", axis=0, tiled=True),
+        jnp.concatenate(
+            lax.all_to_all(jnp.stack([token_tuple[2]] * lax.axis_size("req")), "req", 0, 0), axis=0
+        ),
         lax.all_gather(token_tuple[3], "req", axis=0, tiled=True),
     )
     match = (deal_all[None, :] == mine[:, None]).astype(jnp.bfloat16)

time: 615 us -> 526 us (0.86)
  waiting for transfers between devices: 504 us -> 314 us
  blocking collectives: 33.1 us -> 112 us
  starting transfers between devices: 0.19 us -> 20.3 us
    all_gather x1, waiting for transfers between devices: 136 us -> 14 us  [route_gathered(): lax.all_gather(token_tuple[0], 'req', axis=0, tiled=True)]
    all_gather x1 -> x0, waiting for transfers between devices: 108 us -> none  [route_gathered(): lax.all_gather(token_tuple[2], 'req', axis=0, tiled=True)]
    unnamed x1, blocking collectives: 33.1 us -> 112 us
    all_gather x1, waiting for transfers between devices: 95.3 us -> 136 us  [route_gathered(): lax.all_gather(token_tuple[3], 'req', axis=0, tiled=True)]
    all_to_all x0 -> x1, starting transfers between devices: none -> 20.1 us  [route_gathered(): lax.all_to_all(jnp.stack([token_tuple[2]] * lax.axis_size('req')), 'req',...]
  transfers between devices with their start and end apart: 5 -> 5, of which waited for: 5 -> 4; matrix products, arithmetic and copies ran while one was open for 6% -> 3% of each run, Pallas kernels for 0% -> 0%
where the time goes in v1:
time: 526 us; the launch traced here: 525 us
  waiting for transfers between devices  314 us (60%)
  blocking collectives  112 us (21%)
  matrix products  21.6 us (4%)
  loops' own time  21.3 us (4%)
  starting transfers between devices  20.3 us (4%)
  local copies, waits for them, and re-layouts  15.5 us (3%)
  between operations  14.5 us (3%)
  other arithmetic  6.03 us (1%)
    all_gather x1, waiting for transfers between devices, route_gathered(): lax.all_gather(token_tuple[3], 'req', axis=0, tiled=True)  136 us
    all_gather x1, waiting for transfers between devices, route_gathered(): lax.all_gather(token_tuple[1], 'req', axis=0, tiled=True)  136 us
    unnamed x1, blocking collectives  112 us
    reduce_scatter x1, waiting for transfers between devices, per_device(): lax.psum_scatter(partial_out, 'head', scatter_dimension=1, tiled=True)  25.8 us
    another operation x1, loops' own time, per_device(): lax.scan(advance, (init_states, init_states), (query_seq, forget_seq, val...  21.3 us
    all_to_all x1, starting transfers between devices, route_gathered(): lax.all_to_all(jnp.stack([token_tuple[2]] * lax.axis_size('req')), 'req',...  20.1 us
    dot_general x4, matrix products, route_gathered(): jnp.einsum('rk,kte->rte', match, rows, preferred_element_type=jnp.float32)  15.5 us
    all_gather x1, waiting for transfers between devices, route_gathered(): lax.all_gather(token_tuple[0], 'req', axis=0, tiled=True)  14 us
  transfers between devices with their start and end apart: 5, of which 4 were waited for; matrix products, arithmetic and copies ran while one was open for 3% of the time, Pallas kernels for 0%

profile of v1, /device:TPU:2, one launch (start us, length us, event | category | flops | bytes accessed | tf_op | source)
XLA Modules:
  0.0 525.1 jit_solution(15153452044687888120)
XLA Ops:
  7.2 1.1 copy.69
  8.4 0.7 all-gather.4.cloned.1.call-update
  9.1 2.3 stack.2
  11.4 20.1 %all-to-all-start = ((bf16[128,1,16,512]{3,2,1,0:T(8,128)(2,1)}), bf16[128,1,16,512]{3,2,1,0:T(8,128)(2,1)}, u32[]{:S(2)}, u32[]{:S(2)}) async-start(bf16[128,1,16,512]{3,2,1,0:T(8,128)(2,1)} %stack.2), calls=%async_computation | async-start | bytes 4194304 | tf_op jit(solution)/shard_map/all_to_all | solution.py:16
  31.6 0.7 all-gather.8.cloned.1.call-update
  33.0 1.3 dynamic-slice
  34.3 0.8 dynamic-update-slice
  35.0 112.1 %all-reduce = s32[128]{0:T(128)S(1)} all-reduce(s32[128]{0:T(128)S(1)} %dynamic-update-slice), channel_id=1, replica_groups=mesh['req'=128,'head'=4] {'req'}, use_global_device_ids=true, to_apply=%add | all-reduce | flops 128 | bytes 1024
  147.2 14.0 %all-gather.6.cloned.1.call-done = bf16[128,16,512]{2,1,0:T(8,128)(2,1)} async-done(((bf16[1,16,512]{2,1,0:T(8,128)(2,1)}), bf16[128,16,512]{2,1,0:T(8,128)(2,1)}) %all-gather.6.cloned.1.call-update) | async-done | bytes 2097168 | tf_op jit(solution)/shard_map/all_gather | solution.py:13
  161.2 3.9 fusion.4
  165.1 136.1 %all-gather.4.cloned.1.call-done = bf16[128,16,512]{2,1,0:T(8,128)(2,1)} async-done(((bf16[1,16,512]{2,1,0:T(8,128)(2,1)}), bf16[128,16,512]{2,1,0:T(8,128)(2,1)}) %all-gather.4.cloned.1.call-update) | async-done | bytes 2097168 | tf_op jit(solution)/shard_map/all_gather | solution.py:14
  301.3 3.9 fusion.8
  305.2 136.3 %all-gather.8.cloned.1.call-done = bf16[128,16,512]{2,1,0:T(8,128)(2,1)} async-done(((bf16[1,16,512]{2,1,0:T(8,128)(2,1)}), bf16[128,16,512]{2,1,0:T(8,128)(2,1)}) %all-gather.8.cloned.1.call-update) | async-done | bytes 2097168 | tf_op jit(solution)/shard_map/all_gather | solution.py:18
  441.5 3.9 fusion.2
  445.4 3.9 fusion.6
  449.3 40.8 %while.14 = (s32[]{:T(128)}, f32[1,4,128,128]{3,2,1,0:T(8,128)S(1)}, f32[1,4,128,128]{3,2,1,0:T(8,128)S(1)}, f32[16,1,4,128]{3,2,1,0:T(4,128)S(1)}, f32[16,1,4,1...) while((s32[]{:T(128)}, ...), condition=%wide.region_1.2_spmd, body=%wide.region_0.1_spmd.sunk | while | flops 1049091 | bytes 1339531 | solution.py:73
  449.3 0.6 dynamic_slice.23
  451.5 0.3 fusion.34
  451.8 0.6 dynamic_slice.23
  454.1 0.3 fusion.34
  454.4 0.6 dynamic_slice.23
  456.6 0.3 fusion.34
  456.9 0.6 dynamic_slice.23
  459.2 0.3 fusion.34
  459.5 0.6 dynamic_slice.23
  462.0 0.6 dynamic_slice.23
  464.3 0.3 fusion.34
  464.6 0.6 dynamic_slice.23
  466.8 0.3 fusion.34
  467.1 0.6 dynamic_slice.23
  469.3 0.3 fusion.34
  469.7 0.6 dynamic_slice.23
  471.9 0.3 fusion.34
  472.2 0.6 dynamic_slice.23
  474.4 0.3 fusion.34
  474.8 0.6 dynamic_slice.23
  477.0 0.3 fusion.34
  477.3 0.6 dynamic_slice.23
  479.9 0.6 dynamic_slice.23
  482.1 0.3 fusion.34
  482.4 0.6 dynamic_slice.23
  484.6 0.3 fusion.34
  485.0 0.6 dynamic_slice.23
  487.2 0.3 fusion.34
  487.5 0.6 dynamic_slice.23
  490.3 1.0 fusion.16
  491.3 25.8 %reduce-scatter.2.cloned.1.call-done = f32[16,512]{1,0:T(8,128)} async-done(((f32[16,2048]{1,0:T(8,128)}), f32[16,512]{1,0:T(8,128)}) %reduce-scatter.2.cloned.1.call-update) | async-done | bytes 32784 | tf_op jit(solution)/shard_map/reduce_scatter | solution.py:84
  517.2 1.4 convert_bitcast_fusion
  (110 shorter events, 6.5 us)
Async XLA Ops:
  7.2 483.1 %copy-start = (bf16[512,2048]{1,0:T(8,128)(2,1)S(1)}, bf16[512,2048]{1,0:T(8,128)(2,1)}, u32[]{:S(2)}) copy-start(bf16[512,2048]{1,0:T(8,128)(2,1)} %param.17) | copy-start | bytes 6291460
  7.2 154.0 %all-gather.6.cloned.1.call-start = ((), (), s32[]{:S(2)}) async-start(), calls=%async_computation.3 | async-start | bytes 2113536 | tf_op jit(solution)/shard_map/all_gather | solution.py:13
  8.3 292.9 %all-gather.4.cloned.1.call-start = ((), (), s32[]{:S(2)}) async-start(), calls=%async_computation.2 | async-start | bytes 2113536 | tf_op jit(solution)/shard_map/all_gather | solution.py:14
  11.4 135.8 %copy-start.2 = (f32[128]{0:T(128)S(1)}, f32[128]{0:T(128)}, u32[]{:S(2)}) copy-start(f32[128]{0:T(128)} %param.16) | copy-start | bytes 1540
  11.4 434.0 %all-to-all-start = ((bf16[128,1,16,512]{3,2,1,0:T(8,128)(2,1)}), bf16[128,1,16,512]{3,2,1,0:T(8,128)(2,1)}, u32[]{:S(2)}, u32[]{:S(2)}) async-start(bf16[128,1,16,512]{3,2,1,0:T(8,128)(2,1)} %stack.2), calls=%async_computation | async-start | bytes 4194304 | tf_op jit(solution)/shard_map/all_to_all | solution.py:16
  31.5 410.0 %all-gather.8.cloned.1.call-start = ((), (), s32[]{:S(2)}) async-start(), calls=%async_computation.4 | async-start | bytes 2113536 | tf_op jit(solution)/shard_map/all_gather | solution.py:18
  32.3 484.9 %reduce-scatter.2.cloned.1.call-start = ((), (), s32[]{:S(2)}) async-start(), calls=%async_computation.5 | async-start | bytes 163840 | tf_op jit(solution)/shard_map/reduce_scatter | solution.py:84
  490.1 28.5 %copy-start.1 = (f32[1,4,128,128]{3,2,1,0:T(8,128)}, f32[1,4,128,128]{3,2,1,0:T(8,128)S(1)}, u32[]{:S(2)}) copy-start(f32[1,4,128,128]{3,2,1,0:T(8,128)S(1)} %get-tuple-element.49) | copy-start | bytes 786436
Sparse Core Ops, SparseCore 0:
  11.1 150.0 all-gather.5
  164.4 136.8 all-gather.3
  304.4 137.0 all-gather.7
  491.4 25.6 reduce-scatter.1
